TPU v7x, 256 devices: a whole 4x4x8 slice. The times are simulated.
256 devices in a mesh: pipe: 2 (over core), seq: 4 (over x), tensor: 32 (over z, y).
Axes of the slice: x: 4, y: 4, z: 8, core: 2. Of those that a mesh axis runs over, the one named last changes fastest.
Arguments:
- token_ids: int32 [2, 768], P(None, 'seq'), may hold values from 0 to 511
- embed_table: bfloat16 [512, 8192], P(None, 'tensor'), may hold values from -24 to 24
- in_proj: bfloat16 [2, 8192, 3, 4096], P('pipe', None, None, 'tensor'), may hold values from -0.0625 to 0.0625
- feat_taps: float32 [2, 3, 3, 4096], P('pipe', None, None, 'tensor'), may hold values from -3 to 3
- se_taps: float32 [7, 4096], P(None, 'tensor'), may hold values from -2 to 2
- mr_taps: float32 [128, 4096], P(None, 'tensor'), may hold values from -0.6 to 0.6
- out_proj: bfloat16 [2, 4096, 8192], P('pipe', 'tensor'), may hold values from -0.1875 to 0.1875
- norm_gain: bfloat16 [2, 8192], P('pipe', 'tensor'), may hold values from 0.25 to 1.75
Outputs:
- segment_out: bfloat16 [2, 2, 768, 8192], P('pipe', None, 'seq', 'tensor')
All inputs are finite; a program needn't handle non-finite values.
Results may differ from a plain program's by a relative error of at most 0.023.
Values may be sent and summed in bfloat16 or wider, within the bound.
No kernel may reach another device: no remote copies, remote signals or barrier semaphores. Data moves between devices by JAX's collectives and lax.ppermute only.
A program may use at most 64 MiB of HBM per device.

v0:
```python
import jax
import jax.numpy as jnp
from jax import lax
from jax.sharding import PartitionSpec as P

VOCAB = 512
KL = 128
KS = 7
KF = 3
HALO = KL + KF - 2
epsilon = 1e-06


def swapped(value):
    return lax.ppermute(value, "pipe", [(0, 1), (1, 0)])


def of_section(core, own, other, section):
    return jnp.where(core == section, own, other)


def relaid_out_proj(w_down):
    n_t = lax.axis_size("tensor")
    chan_local, width = w_down.shape
    blocks = w_down.reshape(chan_local, n_t, width // n_t)
    moved = lax.all_to_all(blocks, "tensor", 1, 0, tiled=True)
    return moved.reshape(n_t * chan_local, width // n_t)


def section_step(x_in, w_in, feat, long_taps, w_out, gain):
    rows = x_in.shape[0]
    chan_local = w_in.shape[1] // 3
    aug = jnp.concatenate([x_in, gain.reshape(1, -1).astype(x_in.dtype)], axis=0)
    full = lax.all_gather(aug, "tensor", axis=1, tiled=True)
    values = full[:rows].astype(jnp.float32)
    gain_all = full[rows].astype(jnp.float32)
    inv_rms = lax.rsqrt(jnp.mean(values * values, axis=1, keepdims=True) + epsilon)
    normed = (values * inv_rms * gain_all[None, :]).astype(jnp.bfloat16)
    projected = jnp.dot(normed, w_in, preferred_element_type=jnp.float32).astype(jnp.bfloat16)
    blocks = lax.axis_size("pipe") * lax.axis_size("seq")
    kv_tail = projected[rows - HALO :, chan_local:]
    q_tail = projected[rows - (KF - 1) :, :chan_local]
    kv_prev, q_prev = lax.ppermute(
        (kv_tail, q_tail), ("pipe", "seq"), [(b, b + 1) for b in range(blocks - 1)]
    )
    q_all = jnp.concatenate([q_prev, projected[:, :chan_local]], axis=0).astype(jnp.float32)
    kv_all = jnp.concatenate([kv_prev, projected[:, chan_local:]], axis=0).astype(jnp.float32)
    q_taps = feat[:, 0, :]
    kv_taps = feat[:, 1:, :].reshape(KF, 2 * chan_local)
    kv_span = KL - 1 + rows
    q_feat = jnp.zeros((rows, chan_local), jnp.float32)
    kv_feat = jnp.zeros((kv_span, 2 * chan_local), jnp.float32)
    for tap_index in range(KF):
        offset = KF - 1 - tap_index
        q_feat = q_feat + q_taps[tap_index] * q_all[offset : offset + rows]
        kv_feat = kv_feat + kv_taps[tap_index] * kv_all[offset : offset + kv_span]
    gated_kv = kv_feat[:, :chan_local] * kv_feat[:, chan_local:]

    def add_tap(tap_index, running):
        shifted = lax.dynamic_slice_in_dim(gated_kv, KL - 1 - tap_index, rows, 0)
        return running + long_taps[tap_index] * shifted

    filtered = lax.fori_loop(0, KL, add_tap, jnp.zeros_like(q_feat))
    y_out = (q_feat * filtered).astype(jnp.bfloat16)
    y_full = lax.all_gather(y_out, "tensor", axis=1, tiled=True)
    mixed = jnp.dot(y_full, w_out, preferred_element_type=jnp.float32)
    return (x_in.astype(jnp.float32) + mixed).astype(jnp.bfloat16)


def local(token_ids, embed_table, in_proj, feat_taps, se_taps, mr_taps, out_proj, norm_gain):
    core = lax.axis_index("pipe")
    w_own = in_proj[0].reshape(in_proj.shape[1], -1)
    feat_own = feat_taps[0]
    gain_own = norm_gain[0]
    wt_own = relaid_out_proj(out_proj[0])
    w_other, feat_other, gain_other, wt_other = swapped((w_own, feat_own, gain_own, wt_own))
    padded_se = jnp.concatenate(
        [se_taps, jnp.zeros((KL - KS, se_taps.shape[1]), jnp.float32)], axis=0
    )
    filters = (padded_se, mr_taps)
    ids = lax.dynamic_index_in_dim(token_ids, core, 0, keepdims=False)
    vocab_ids = jnp.arange(VOCAB, dtype=jnp.int32)
    one_hot = (ids[:, None] == vocab_ids[None, :]).astype(jnp.bfloat16)
    current = jnp.dot(one_hot, embed_table, preferred_element_type=jnp.float32).astype(jnp.bfloat16)
    results = []
    for section in range(2):
        current = section_step(
            current,
            of_section(core, w_own, w_other, section),
            of_section(core, feat_own, feat_other, section),
            filters[section],
            of_section(core, wt_own, wt_other, section),
            of_section(core, gain_own, gain_other, section),
        )
        results.append(current)
    first_mine, second_mine = results
    second_slice_of_first = lax.ppermute(first_mine, "pipe", [(1, 0)])
    first_slice_of_second = lax.ppermute(second_mine, "pipe", [(0, 1)])
    lead = core == 0
    slice_zero = jnp.where(lead, first_mine, first_slice_of_second)
    slice_one = jnp.where(lead, second_slice_of_first, second_mine)
    return jnp.stack([slice_zero, slice_one], axis=0)[None]


def solution(mesh):
    return jax.shard_map(
        local,
        mesh=mesh,
        in_specs=(
            P(None, "seq"),
            P(None, "tensor"),
            P("pipe", None, None, "tensor"),
            P("pipe", None, None, "tensor"),
            P(None, "tensor"),
            P(None, "tensor"),
            P("pipe", "tensor", None),
            P("pipe", "tensor"),
        ),
        out_specs=P("pipe", None, "seq", "tensor"),
        check_vma=False,
    )
```

profile of v0, /device:TPU:1, one launch (start us, length us, event | category | flops | bytes accessed | tf_op | source)
XLA Modules:
  0.0 497.7 jit_solution(15193292453883227668)
XLA Ops:
  6.5 0.7 reduce
  7.3 3.3 collective-permute-start.1
  12.3 8.9 %copy.10 = bf16[1,8192,3,128]{1,3,2,0:T(8,128)(2,1)} copy(bf16[1,8192,3,128]{3,1,2,0:T(8,128)(2,1)} %param.14) | data formatting | bytes 12582912 | tf_op args[2]
  21.7 2.4 copy.11
  24.1 9.5 %all-to-all-start = ((bf16[128,32,256]{0,2,1:T(8,128)(2,1)}), bf16[128,32,256]{0,2,1:T(8,128)(2,1)S(1)}, u32[]{:S(2)}, u32[]{:S(2)}) async-start(bf16[128,32,256]{0,2,1:T(8,128)(2,1)} %bitcast.58), calls=%async_computation | async-start | bytes 4194304 | tf_op jit(solution)/shard_map/all_to_all | solution.py:26
  33.7 75.9 %all-gather.5.cloned.1.call-done = bf16[193,8192]{1,0:T(8,128)(2,1)} async-done(((bf16[193,256]{1,0:T(8,128)(2,1)}), bf16[193,8192]{1,0:T(8,128)(2,1)}) %all-gather.5.cloned.1.call-update) | async-done | bytes 3162128 | tf_op jit(solution)/shard_map/all_gather | solution.py:34
  109.6 2.6 fusion
  112.2 0.9 slice_convert_fusion.1
  113.1 6.0 %fusion.26 = bf16[192,384]{1,0:T(8,128)(2,1)S(1)} fusion(bf16[8192,384]{0,1:T(8,128)(2,1)} %bitcast.60, bf16[8192,384]{0,1:T(8,128)(2,1)} %collective-permute-done.2, pred[]{:T(512)S(6)} %eq.12, f32[8192]{0:T(1024)S(1)} %bitcast.65, f32[192]{0:T(256)S(1)} %add_rsqrt_fusion.1, bf16[193,8192]{1,0:T(8,128)(2,1)} %all-gather.5.cloned.1.call-done), kind=kOutput, calls=%fused_computation.32 | convolution fusion | flops 1217470464 | bytes 15909633 | tf_op jit(solution)/shard_map/dot_general | solution.py:39
  119.1 3.1 collective-permute-start.3
  122.3 3.0 collective-permute-start.4
  125.3 2.7 collective-permute-done.3
  128.1 2.7 collective-permute-done.4
  131.0 10.6 %while.32 = (s32[]{:T(128)}, f32[192,128]{1,0:T(8,128)S(1)}, f32[128,128]{1,0:T(8,128)S(1)}, f32[319,128]{1,0:T(8,128)S(1)}, s32[]{:T(128)}, /*index=5*/s32[]{:T(128)}, s32[]{:T(128)}, s32[]{:T(128)}) while((s32[]{:T(128)}, f32[192,128]{1,0:T(8,128)S(1)}, f32[128,128]{1,0:T(8,128)S(1)}, f32[319,128]{1,0:T(8,128)S(1)}, s32[]{:T(128)}, ...), condition=%wide.region_2.3_spmd.clone, body=%wide.region_1.2_spmd.clone.sunk | while | flops 73735 | bytes 296597 | solution.py:63
  142.4 2.9 copy.12
  145.8 4.0 collective-permute-done.5
  149.8 60.7 %all-gather.7.cloned.1.call-done = bf16[192,4096]{1,0:T(8,128)(2,1)} async-done(((bf16[192,128]{1,0:T(8,128)(2,1)}), bf16[192,4096]{1,0:T(8,128)(2,1)}) %all-gather.7.cloned.1.call-update) | async-done | bytes 1572880 | tf_op jit(solution)/shard_map/all_gather | solution.py:65
  210.5 2.0 fusion.39
  213.3 80.0 %all-gather.9.cloned.1.call-done = bf16[193,8192]{1,0:T(8,128)(2,1)} async-done(((bf16[193,256]{1,0:T(8,128)(2,1)}), bf16[193,8192]{1,0:T(8,128)(2,1)}) %all-gather.9.cloned.1.call-update) | async-done | bytes 3162128 | tf_op jit(solution)/shard_map/all_gather | solution.py:34
  293.3 2.6 fusion.3
  295.9 0.9 slice_convert_fusion
  296.8 6.0 %fusion.31 = bf16[192,384]{1,0:T(8,128)(2,1)S(1)} fusion(bf16[8192,384]{0,1:T(8,128)(2,1)} %bitcast.61, bf16[8192,384]{0,1:T(8,128)(2,1)} %collective-permute-done.2, pred[]{:T(512)S(6)} %eq.33, f32[8192]{0:T(1024)S(1)} %bitcast.66, f32[192]{0:T(256)S(1)} %add_rsqrt_fusion, bf16[193,8192]{1,0:T(8,128)(2,1)} %all-gather.9.cloned.1.call-done), kind=kOutput, calls=%fused_computation.33 | convolution fusion | flops 1217470464 | bytes 15909633 | tf_op jit(solution)/shard_map/dot_general | solution.py:39
  302.8 3.2 collective-permute-start.6
  306.1 3.1 collective-permute-start.7
  309.2 2.2 collective-permute-done.6
  311.5 2.7 collective-permute-done.7
  314.4 96.0 %while.33 = (s32[]{:T(128)}, f32[192,128]{1,0:T(8,128)S(1)}, f32[128,128]{1,0:T(8,128)}, f32[319,128]{1,0:T(8,128)S(1)}, s32[]{:T(128)}, /*index=5*/s32[]{:T(128)}, s32[]{:T(128)}, s32[]{:T(128)}) while((s32[]{:T(128)}, f32[192,128]{1,0:T(8,128)S(1)}, f32[128,128]{1,0:T(8,128)}, f32[319,128]{1,0:T(8,128)S(1)}, s32[]{:T(128)}, ...), condition=%wide.region_5.6_spmd.clone, body=%wide.region_4.5_spmd.clone.sunk | while | flops 73735 | bytes 296597 | solution.py:63
  411.1 2.5 collective-permute-start.9
  413.6 68.0 %all-gather.11.cloned.1.call-done = bf16[192,4096]{1,0:T(8,128)(2,1)} async-done(((bf16[192,128]{1,0:T(8,128)(2,1)}), bf16[192,4096]{1,0:T(8,128)(2,1)}) %all-gather.11.cloned.1.call-update) | async-done | bytes 1572880 | tf_op jit(solution)/shard_map/all_gather | solution.py:65
  481.6 2.0 fusion.20
  483.7 1.3 collective-permute-start.8
  485.0 5.4 %collective-permute-done.8 = bf16[192,256]{1,0:T(8,128)(2,1)S(1)} collective-permute-done((bf16[192,256]{1,0:T(8,128)(2,1)S(1)}, bf16[192,256]{1,0:T(8,128)(2,1)S(1)}, u32[]{:S(2)}, u32[]{:S(2)}) %collective-permute-start.8) | collective-permute-done | bytes 98336 | tf_op jit(solution)/shard_map/ppermute | solution.py:98
  (579 shorter events, 104.6 us)
Async XLA Ops:
  6.5 4.7 copy-start
  6.5 103.0 %all-gather.5.cloned.1.call-start = ((), (), s32[]{:S(2)}) async-start(), calls=%async_computation.1 | async-start | bytes 3379200 | tf_op jit(solution)/shard_map/all_gather | solution.py:34
  7.3 4.3 collective-permute-start.1
  12.3 9.0 %copy-start.3 = (f32[1,3,3,128]{3,0,2,1:T(1,128)S(1)}, f32[1,3,3,128]{3,0,2,1:T(1,128)}, u32[]{:S(2)}) copy-start(f32[1,3,3,128]{3,0,2,1:T(1,128)} %param.15) | copy-start | bytes 13828
  12.3 9.4 %copy-start.1 = (bf16[1,128,8192]{2,1,0:T(8,128)(2,1)S(1)}, bf16[1,128,8192]{2,1,0:T(8,128)(2,1)}, u32[]{:S(2)}) copy-start(bf16[1,128,8192]{2,1,0:T(8,128)(2,1)} %param.18) | copy-start | bytes 6291460
  21.1 92.0 %collective-permute-start.2 = (bf16[8192,384]{0,1:T(8,128)(2,1)}, bf16[8192,384]{0,1:T(8,128)(2,1)}, u32[]{:S(2)}, u32[]{:S(2)}) collective-permute-start(bf16[8192,384]{0,1:T(8,128)(2,1)} %bitcast.59), channel_id=1, source_target_pairs={{0,128},{128,0},{1,129},{129,1},{2,130},{130,2},{3,131},{131,3},{4... | collective-permute-start | bytes 18874376 | tf_op jit(solution)/shard_map/ppermute | solution.py:15
  21.3 12.4 %copy-start.4 = (f32[7,128]{1,0:T(8,128)S(1)}, f32[7,128]{1,0:T(8,128)}, u32[]{:S(2)}) copy-start(f32[7,128]{1,0:T(8,128)} %param.16) | copy-start | bytes 10756
  21.3 12.4 %collective-permute-start = (f32[3,3,128]{2,1,0:T(4,128)S(1)}, f32[3,3,128]{2,1,0:T(4,128)S(1)}, u32[]{:S(2)}, u32[]{:S(2)}) collective-permute-start(f32[3,3,128]{2,1,0:T(4,128)S(1)} %bitcast.67), channel_id=1, source_target_pairs={{0,128},{128,0},{1,129},{129,1},{2,130},{130,2},{3,131},{131,3},{4... | collective-permute-start | bytes 13832 | tf_op jit(solution)/shard_map/ppermute | solution.py:15
  24.1 118.2 %all-to-all-start = ((bf16[128,32,256]{0,2,1:T(8,128)(2,1)}), bf16[128,32,256]{0,2,1:T(8,128)(2,1)S(1)}, u32[]{:S(2)}, u32[]{:S(2)}) async-start(bf16[128,32,256]{0,2,1:T(8,128)(2,1)} %bitcast.58), calls=%async_computation | async-start | bytes 4194304 | tf_op jit(solution)/shard_map/all_to_all | solution.py:26
  33.6 176.9 %all-gather.7.cloned.1.call-start = ((), (), s32[]{:S(2)}) async-start(), calls=%async_computation.2 | async-start | bytes 1622016 | tf_op jit(solution)/shard_map/all_gather | solution.py:65
  119.1 8.9 %collective-permute-start.3 = (bf16[2,128]{1,0:T(2,128)(2,1)S(1)}, bf16[2,128]{1,0:T(2,128)(2,1)S(1)}, u32[]{:S(2)}, u32[]{:S(2)}) collective-permute-start(bf16[2,128]{1,0:T(2,128)(2,1)S(1)} %slice.191), channel_id=1, source_target_pairs={{0,32},{32,64},{64,96},{96,128},{128,160},{160,192},{192,224},{1,3... | collective-permute-start | bytes 1544 | tf_op jit(solution)/shard_map/ppermute | solution.py:43
  122.3 8.5 %collective-permute-start.4 = (bf16[129,256]{1,0:T(8,128)(2,1)S(1)}, bf16[129,256]{1,0:T(8,128)(2,1)S(1)}, u32[]{:S(2)}, u32[]{:S(2)}) collective-permute-start(bf16[129,256]{1,0:T(8,128)(2,1)S(1)} %slice.199), channel_id=1, source_target_pairs={{0,32},{32,64},{64,96},{96,128},{128,160},{160,192},{192,224},{1,3... | collective-permute-start | bytes 198152 | tf_op jit(solution)/shard_map/ppermute | solution.py:43
  142.3 151.0 %all-gather.9.cloned.1.call-start = ((), (), s32[]{:S(2)}) async-start(), calls=%async_computation.3 | async-start | bytes 3379200 | tf_op jit(solution)/shard_map/all_gather | solution.py:34
  145.3 4.5 collective-permute-start.5
  149.8 62.7 %copy-start.5 = (bf16[4096,256]{1,0:T(8,128)(2,1)}, bf16[4096,256]{1,0:T(8,128)(2,1)S(1)}, u32[]{:S(2)}) copy-start(bf16[4096,256]{1,0:T(8,128)(2,1)S(1)} %collective-permute-done.5) | copy-start | bytes 6291460
  213.2 268.4 %all-gather.11.cloned.1.call-start = ((), (), s32[]{:S(2)}) async-start(), calls=%async_computation.4 | async-start | bytes 1622016 | tf_op jit(solution)/shard_map/all_gather | solution.py:65
  302.8 178.8 %copy-start.2 = (bf16[32,128,1,256]{3,1,0,2:T(8,128)(2,1)S(1)}, bf16[32,128,1,256]{3,1,0,2:T(8,128)(2,1)}, u32[]{:S(2)}) copy-start(bf16[32,128,1,256]{3,1,0,2:T(8,128)(2,1)} %copy.12) | copy-start | bytes 6291460
  302.8 8.6 %collective-permute-start.6 = (bf16[2,128]{1,0:T(2,128)(2,1)S(1)}, bf16[2,128]{1,0:T(2,128)(2,1)S(1)}, u32[]{:S(2)}, u32[]{:S(2)}) collective-permute-start(bf16[2,128]{1,0:T(2,128)(2,1)S(1)} %slice.211), channel_id=1, source_target_pairs={{0,32},{32,64},{64,96},{96,128},{128,160},{160,192},{192,224},{1,3... | collective-permute-start | bytes 1544 | tf_op jit(solution)/shard_map/ppermute | solution.py:43
  306.1 8.1 %collective-permute-start.7 = (bf16[129,256]{1,0:T(8,128)(2,1)S(1)}, bf16[129,256]{1,0:T(8,128)(2,1)S(1)}, u32[]{:S(2)}, u32[]{:S(2)}) collective-permute-start(bf16[129,256]{1,0:T(8,128)(2,1)S(1)} %slice.219), channel_id=1, source_target_pairs={{0,32},{32,64},{64,96},{96,128},{128,160},{160,192},{192,224},{1,3... | collective-permute-start | bytes 198152 | tf_op jit(solution)/shard_map/ppermute | solution.py:43
  411.1 72.6 %collective-permute-start.9 = (bf16[192,256]{1,0:T(8,128)(2,1)S(1)}, bf16[192,256]{1,0:T(8,128)(2,1)S(1)}, u32[]{:S(2)}, u32[]{:S(2)}) collective-permute-start(bf16[192,256]{1,0:T(8,128)(2,1)S(1)} %fusion.39), channel_id=1, source_target_pairs={{128,0},{129,1},{130,2},{131,3},{132,4},{133,5},{134,6},{135,7},{1... | collective-permute-start | bytes 294920 | tf_op jit(solution)/shard_map/ppermute | solution.py:97
  483.7 6.7 %collective-permute-start.8 = (bf16[192,256]{1,0:T(8,128)(2,1)S(1)}, bf16[192,256]{1,0:T(8,128)(2,1)S(1)}, u32[]{:S(2)}, u32[]{:S(2)}) collective-permute-start(bf16[192,256]{1,0:T(8,128)(2,1)S(1)} %get-tuple-element.274), channel_id=1, source_target_pairs={{0,128},{1,129},{2,130},{3,131},{4,132},{5,133},{6,134},{7,135},{8... | collective-permute-start | bytes 294920 | tf_op jit(solution)/shard_map/ppermute | solution.py:98
Sparse Core Ops, SparseCore 0:
  12.4 97.1 all-gather.4
  142.4 68.0 all-gather.6
  213.3 79.9 all-gather.8
  411.2 70.3 all-gather.10
where the time goes:
time: 502 us; the launch traced here: 498 us
  waiting for transfers between devices  305 us (61%)
  local copies, waits for them, and re-layouts  105 us (21%)
  starting transfers between devices  30.1 us (6%)
  other arithmetic  19.8 us (4%)
  matrix products  16.2 us (3%)
  between operations  13.5 us (3%)
  loops' own time  8.15 us (2%)
    all_gather x2, waiting for transfers between devices, section_step(): full = lax.all_gather(aug, 'tensor', axis=1, tiled=True)  156 us
    all_gather x2, waiting for transfers between devices, section_step(): y_full = lax.all_gather(y_out, 'tensor', axis=1, tiled=True)  129 us
    mul x256, local copies, waits for them, and re-layouts, add_tap(): return running + long_taps[tap_index] * shifted  90.3 us
    ppermute x4, starting transfers between devices, section_step(): lax.ppermute((kv_tail, q_tail), ('pipe', 'seq'), [(b, b + 1) for b in ran...  12.4 us
    dot_general x2, matrix products, section_step(): jnp.dot(normed, w_in, preferred_element_type=jnp.float32)  12 us
    unnamed x15, local copies, waits for them, and re-layouts  11.3 us
    ppermute x4, waiting for transfers between devices, section_step(): lax.ppermute((kv_tail, q_tail), ('pipe', 'seq'), [(b, b + 1) for b in ran...  10.5 us
  transfers between devices with their start and end apart: 15, of which 10 were waited for; matrix products, arithmetic and copies ran while one was open for 7% of the time, Pallas kernels for 0%

commit v1 on v0

--- a/solution.py
+++ b/solution.py
@@ -31,7 +31,10 @@
     rows = x_in.shape[0]
     chan_local = w_in.shape[1] // 3
     aug = jnp.concatenate([x_in, gain.reshape(1, -1).astype(x_in.dtype)], axis=0)
-    full = lax.all_gather(aug, "tensor", axis=1, tiled=True)
+    full = jnp.concatenate(
+        jax.lax.all_to_all(jnp.stack(jax.lax.psum(1, "tensor") * [aug], axis=0), "tensor", 0, 0),
+        axis=1,
+    )
     values = full[:rows].astype(jnp.float32)
     gain_all = full[rows].astype(jnp.float32)
     inv_rms = lax.rsqrt(jnp.mean(values * values, axis=1, keepdims=True) + epsilon)

time: 502 us -> 583 us (1.16)
  local copies, waits for them, and re-layouts: 105 us -> 202 us
  waiting for transfers between devices: 305 us -> 280 us
  starting transfers between devices: 30.1 us -> 44.8 us
  other arithmetic: 19.8 us -> 13.9 us
    all_gather x2 -> x0, waiting for transfers between devices: 156 us -> none  [section_step(): full = lax.all_gather(aug, 'tensor', axis=1, tiled=True)]
    all_to_all x0 -> x2, waiting for transfers between devices: none -> 127 us  [section_step(): jax.lax.all_to_all(jnp.stack(jax.lax.psum(1, 'tensor') * [aug], axis=0),...]
    mul x256, local copies, waits for them, and re-layouts: 90.3 us -> 177 us  [add_tap(): return running + long_taps[tap_index] * shifted]
    all_to_all x0 -> x2, starting transfers between devices: none -> 16.4 us  [section_step(): jax.lax.all_to_all(jnp.stack(jax.lax.psum(1, 'tensor') * [aug], axis=0),...]
    ppermute x4, waiting for transfers between devices: 10.5 us -> 18.2 us  [section_step(): lax.ppermute((kv_tail, q_tail), ('pipe', 'seq'), [(b, b + 1) for b in ran...]
    unnamed x15 -> x31, local copies, waits for them, and re-layouts: 11.3 us -> 15 us
  transfers between devices with their start and end apart: 15 -> 15, of which waited for: 10 -> 11; matrix products, arithmetic and copies ran while one was open for 7% -> 21% of each run, Pallas kernels for 0% -> 0%
where the time goes in v1:
time: 583 us; the launch traced here: 574 us
  waiting for transfers between devices  280 us (48%)
  local copies, waits for them, and re-layouts  202 us (35%)
  starting transfers between devices  44.8 us (8%)
  between operations  14 us (2%)
  other arithmetic  13.9 us (2%)
  matrix products  12.5 us (2%)
  loops' own time  6.6 us (1%)
    mul x256, local copies, waits for them, and re-layouts, add_tap(): return running + long_taps[tap_index] * shifted  177 us
    all_to_all x2, waiting for transfers between devices, section_step(): jax.lax.all_to_all(jnp.stack(jax.lax.psum(1, 'tensor') * [aug], axis=0),...  127 us
    all_gather x2, waiting for transfers between devices, section_step(): y_full = lax.all_gather(y_out, 'tensor', axis=1, tiled=True)  124 us
    ppermute x4, waiting for transfers between devices, section_step(): lax.ppermute((kv_tail, q_tail), ('pipe', 'seq'), [(b, b + 1) for b in ran...  18.2 us
    all_to_all x2, starting transfers between devices, section_step(): jax.lax.all_to_all(jnp.stack(jax.lax.psum(1, 'tensor') * [aug], axis=0),...  16.4 us
    unnamed x31, local copies, waits for them, and re-layouts  15 us
    ppermute x4, starting transfers between devices, section_step(): lax.ppermute((kv_tail, q_tail), ('pipe', 'seq'), [(b, b + 1) for b in ran...  12.6 us
  transfers between devices with their start and end apart: 15, of which 11 were waited for; matrix products, arithmetic and copies ran while one was open for 21% of the time, Pallas kernels for 0%

profile of v1, /device:TPU:1, one launch (start us, length us, event | category | flops | bytes accessed | tf_op | source)
XLA Modules:
  0.0 573.6 jit_solution(5851409230591181254)
XLA Ops:
  7.3 3.3 collective-permute-start.1
  11.6 1.9 stack.10
  13.5 9.5 %all-to-all-start = ((bf16[32,193,256]{2,1,0:T(8,128)(2,1)}), bf16[32,193,256]{2,1,0:T(8,128)(2,1)S(1)}, u32[]{:S(2)}, u32[]{:S(2)}) async-start(bf16[32,193,256]{2,1,0:T(8,128)(2,1)} %stack.10), calls=%async_computation | async-start | bytes 6553600 | tf_op jit(solution)/shard_map/all_to_all | solution.py:35
  23.0 8.6 %copy.14 = bf16[1,8192,3,128]{1,3,2,0:T(8,128)(2,1)} copy(bf16[1,8192,3,128]{3,1,2,0:T(8,128)(2,1)} %param.14) | data formatting | bytes 12582912 | tf_op args[2]
  32.1 4.1 copy.15
  37.1 59.6 %all-to-all-done = bf16[32,193,256]{2,1,0:T(8,128)(2,1)S(1)} async-done(((bf16[32,193,256]{2,1,0:T(8,128)(2,1)}), bf16[32,193,256]{2,1,0:T(8,128)(2,1)S(1)}, u32[]{:S(2)}, u32[]{:S(2)}) %all-to-all-start) | async-done | bytes 3162144 | tf_op jit(solution)/shard_map/all_to_all | solution.py:35
  96.7 7.7 %all-to-all-start.1 = ((bf16[128,32,256]{0,2,1:T(8,128)(2,1)}), bf16[128,32,256]{0,2,1:T(8,128)(2,1)}, u32[]{:S(2)}, u32[]{:S(2)}) async-start(bf16[128,32,256]{0,2,1:T(8,128)(2,1)} %bitcast.71), calls=%async_computation.1 | async-start | bytes 4194304 | tf_op jit(solution)/shard_map/all_to_all | solution.py:26
  105.3 0.8 copy.19
  107.6 5.2 fusion.18
  112.8 3.1 collective-permute-start.3
  116.0 3.1 collective-permute-start.4
  119.3 3.9 collective-permute-done.4
  123.4 95.2 %while.32 = (s32[]{:T(128)}, f32[192,128]{1,0:T(8,128)S(1)}, f32[128,128]{1,0:T(8,128)}, f32[319,128]{1,0:T(8,128)S(1)}, s32[]{:T(128)}, /*index=5*/s32[]{:T(128)}, s32[]{:T(128)}, s32[]{:T(128)}) while((s32[]{:T(128)}, f32[192,128]{1,0:T(8,128)S(1)}, f32[128,128]{1,0:T(8,128)}, f32[319,128]{1,0:T(8,128)S(1)}, s32[]{:T(128)}, ...), condition=%wide.region_2.3_spmd.clone, body=%wide.region_1.2_spmd.clone.sunk | while | flops 73735 | bytes 296605 | solution.py:66
  219.3 3.3 copy.16
  222.7 4.3 collective-permute-done.5
  226.9 60.2 %all-gather.3.cloned.1.call-done = bf16[192,4096]{1,0:T(8,128)(2,1)} async-done(((bf16[192,128]{1,0:T(8,128)(2,1)}), bf16[192,4096]{1,0:T(8,128)(2,1)}) %all-gather.3.cloned.1.call-update) | async-done | bytes 1572880 | tf_op jit(solution)/shard_map/all_gather | solution.py:68
  287.1 2.7 fusion.27
  289.8 1.9 stack.11
  291.7 6.9 %all-to-all-start.2 = ((bf16[32,193,256]{2,1,0:T(8,128)(2,1)}), bf16[32,193,256]{2,1,0:T(8,128)(2,1)S(1)}, u32[]{:S(2)}, u32[]{:S(2)}) async-start(bf16[32,193,256]{2,1,0:T(8,128)(2,1)} %stack.11), calls=%async_computation.2 | async-start | bytes 6553600 | tf_op jit(solution)/shard_map/all_to_all | solution.py:35
  298.9 67.5 %all-to-all-done.2 = bf16[32,193,256]{2,1,0:T(8,128)(2,1)S(1)} async-done(((bf16[32,193,256]{2,1,0:T(8,128)(2,1)}), bf16[32,193,256]{2,1,0:T(8,128)(2,1)S(1)}, u32[]{:S(2)}, u32[]{:S(2)}) %all-to-all-start.2) | async-done | bytes 3162144 | tf_op jit(solution)/shard_map/all_to_all | solution.py:35
  369.4 0.9 slice-done.3
  370.3 2.4 fusion.21
  372.7 3.2 collective-permute-start.6
  376.0 3.1 collective-permute-start.7
  379.1 11.4 %collective-permute-done.6 = bf16[2,128]{1,0:T(2,128)(2,1)S(1)} collective-permute-done((bf16[2,128]{1,0:T(2,128)(2,1)S(1)}, bf16[2,128]{1,0:T(2,128)(2,1)S(1)}, u32[]{:S(2)}, u32[]{:S(2)}) %collective-permute-start.6) | collective-permute-done | bytes 544 | tf_op jit(solution)/shard_map/ppermute | solution.py:46
  390.5 2.7 collective-permute-done.7
  393.4 96.5 %while.33 = (s32[]{:T(128)}, f32[192,128]{1,0:T(8,128)S(1)}, f32[128,128]{1,0:T(8,128)}, f32[319,128]{1,0:T(8,128)S(1)}, s32[]{:T(128)}, /*index=5*/s32[]{:T(128)}, s32[]{:T(128)}, s32[]{:T(128)}) while((s32[]{:T(128)}, f32[192,128]{1,0:T(8,128)S(1)}, f32[128,128]{1,0:T(8,128)}, f32[319,128]{1,0:T(8,128)S(1)}, s32[]{:T(128)}, ...), condition=%wide.region_5.6_spmd.clone, body=%wide.region_4.5_spmd.clone.sunk | while | flops 73735 | bytes 296605 | solution.py:66
  490.7 2.6 collective-permute-start.9
  493.3 63.9 %all-gather.5.cloned.1.call-done = bf16[192,4096]{1,0:T(8,128)(2,1)} async-done(((bf16[192,128]{1,0:T(8,128)(2,1)}), bf16[192,4096]{1,0:T(8,128)(2,1)}) %all-gather.5.cloned.1.call-update) | async-done | bytes 1572880 | tf_op jit(solution)/shard_map/all_gather | solution.py:68
  557.2 2.0 fusion.12
  559.3 1.3 collective-permute-start.8
  560.6 5.4 collective-permute-done.8
  (601 shorter events, 196.5 us)
Async XLA Ops:
  6.5 4.7 copy-start
  7.3 4.3 collective-permute-start.1
  11.5 1.9 copy-start.6
  13.5 83.3 %all-to-all-start = ((bf16[32,193,256]{2,1,0:T(8,128)(2,1)}), bf16[32,193,256]{2,1,0:T(8,128)(2,1)S(1)}, u32[]{:S(2)}, u32[]{:S(2)}) async-start(bf16[32,193,256]{2,1,0:T(8,128)(2,1)} %stack.10), calls=%async_computation | async-start | bytes 6553600 | tf_op jit(solution)/shard_map/all_to_all | solution.py:35
  23.0 9.1 %copy-start.8 = (f32[1,3,3,128]{3,0,2,1:T(1,128)S(1)}, f32[1,3,3,128]{3,0,2,1:T(1,128)}, u32[]{:S(2)}) copy-start(f32[1,3,3,128]{3,0,2,1:T(1,128)} %param.15) | copy-start | bytes 13828
  31.6 4.6 copy-start.9
  31.6 75.3 %collective-permute-start.2 = (bf16[8192,384]{0,1:T(8,128)(2,1)}, bf16[8192,384]{0,1:T(8,128)(2,1)}, u32[]{:S(2)}, u32[]{:S(2)}) collective-permute-start(bf16[8192,384]{0,1:T(8,128)(2,1)} %bitcast.72), channel_id=1, source_target_pairs={{0,128},{128,0},{1,129},{129,1},{2,130},{130,2},{3,131},{131,3},{4... | collective-permute-start | bytes 18874376 | tf_op jit(solution)/shard_map/ppermute | solution.py:15
  32.0 5.1 collective-permute-start
  96.7 122.5 %all-to-all-start.1 = ((bf16[128,32,256]{0,2,1:T(8,128)(2,1)}), bf16[128,32,256]{0,2,1:T(8,128)(2,1)}, u32[]{:S(2)}, u32[]{:S(2)}) async-start(bf16[128,32,256]{0,2,1:T(8,128)(2,1)} %bitcast.71), calls=%async_computation.1 | async-start | bytes 4194304 | tf_op jit(solution)/shard_map/all_to_all | solution.py:26
  104.5 182.7 %all-gather.3.cloned.1.call-start = ((), (), s32[]{:S(2)}) async-start(), calls=%async_computation.3 | async-start | bytes 1622016 | tf_op jit(solution)/shard_map/all_gather | solution.py:68
  104.5 2.3 slice-start
  105.3 2.3 slice-start.1
  112.8 6.5 %collective-permute-start.3 = (bf16[2,128]{1,0:T(2,128)(2,1)S(1)}, bf16[2,128]{1,0:T(2,128)(2,1)S(1)}, u32[]{:S(2)}, u32[]{:S(2)}) collective-permute-start(bf16[2,128]{1,0:T(2,128)(2,1)S(1)} %slice.195), channel_id=1, source_target_pairs={{0,32},{32,64},{64,96},{96,128},{128,160},{160,192},{192,224},{1,3... | collective-permute-start | bytes 1544 | tf_op jit(solution)/shard_map/ppermute | solution.py:46
  116.0 7.2 %collective-permute-start.4 = (bf16[129,256]{1,0:T(8,128)(2,1)S(1)}, bf16[129,256]{1,0:T(8,128)(2,1)S(1)}, u32[]{:S(2)}, u32[]{:S(2)}) collective-permute-start(bf16[129,256]{1,0:T(8,128)(2,1)S(1)} %slice.203), channel_id=1, source_target_pairs={{0,32},{32,64},{64,96},{96,128},{128,160},{160,192},{192,224},{1,3... | collective-permute-start | bytes 198152 | tf_op jit(solution)/shard_map/ppermute | solution.py:46
  123.4 163.7 %copy-start.7 = (bf16[192,256]{1,0:T(8,128)(2,1)S(1)}, bf16[192,256]{1,0:T(8,128)(2,1)}, u32[]{:S(2)}) copy-start(bf16[192,256]{1,0:T(8,128)(2,1)} %copy-done.6) | copy-start | bytes 294916
  222.6 67.3 %copy-start.2 = (bf16[32,128,1,256]{3,1,0,2:T(8,128)(2,1)}, bf16[32,128,1,256]{3,1,0,2:T(8,128)(2,1)S(1)}, u32[]{:S(2)}) copy-start(bf16[32,128,1,256]{3,1,0,2:T(8,128)(2,1)S(1)} %copy.16) | copy-start | bytes 6291460
  222.6 4.4 collective-permute-start.5
  289.8 1.9 copy-start.4
  291.7 74.7 %all-to-all-start.2 = ((bf16[32,193,256]{2,1,0:T(8,128)(2,1)}), bf16[32,193,256]{2,1,0:T(8,128)(2,1)S(1)}, u32[]{:S(2)}, u32[]{:S(2)}) async-start(bf16[32,193,256]{2,1,0:T(8,128)(2,1)} %stack.11), calls=%async_computation.2 | async-start | bytes 6553600 | tf_op jit(solution)/shard_map/all_to_all | solution.py:35
  298.7 258.6 %all-gather.5.cloned.1.call-start = ((), (), s32[]{:S(2)}) async-start(), calls=%async_computation.4 | async-start | bytes 1622016 | tf_op jit(solution)/shard_map/all_gather | solution.py:68
  367.2 2.2 slice-start.2
  368.0 2.3 slice-start.3
  372.7 118.0 %copy-start.5 = (bf16[192,256]{1,0:T(8,128)(2,1)S(1)}, bf16[192,256]{1,0:T(8,128)(2,1)}, u32[]{:S(2)}) copy-start(bf16[192,256]{1,0:T(8,128)(2,1)} %copy-done.4) | copy-start | bytes 294916
  372.7 184.6 %copy-start.3 = (bf16[32,128,1,256]{3,1,0,2:T(8,128)(2,1)S(1)}, bf16[32,128,1,256]{3,1,0,2:T(8,128)(2,1)}, u32[]{:S(2)}) copy-start(bf16[32,128,1,256]{3,1,0,2:T(8,128)(2,1)} %copy-done.2) | copy-start | bytes 6291460
  372.7 17.8 %collective-permute-start.6 = (bf16[2,128]{1,0:T(2,128)(2,1)S(1)}, bf16[2,128]{1,0:T(2,128)(2,1)S(1)}, u32[]{:S(2)}, u32[]{:S(2)}) collective-permute-start(bf16[2,128]{1,0:T(2,128)(2,1)S(1)} %slice.215), channel_id=1, source_target_pairs={{0,32},{32,64},{64,96},{96,128},{128,160},{160,192},{192,224},{1,3... | collective-permute-start | bytes 1544 | tf_op jit(solution)/shard_map/ppermute | solution.py:46
  376.0 17.2 %collective-permute-start.7 = (bf16[129,256]{1,0:T(8,128)(2,1)S(1)}, bf16[129,256]{1,0:T(8,128)(2,1)S(1)}, u32[]{:S(2)}, u32[]{:S(2)}) collective-permute-start(bf16[129,256]{1,0:T(8,128)(2,1)S(1)} %slice.223), channel_id=1, source_target_pairs={{0,32},{32,64},{64,96},{96,128},{128,160},{160,192},{192,224},{1,3... | collective-permute-start | bytes 198152 | tf_op jit(solution)/shard_map/ppermute | solution.py:46
  490.7 76.1 %copy-start.1 = (bf16[512,256]{1,0:T(8,128)(2,1)S(1)}, bf16[512,256]{1,0:T(8,128)(2,1)}, u32[]{:S(2)}) copy-start(bf16[512,256]{1,0:T(8,128)(2,1)} %param.13) | copy-start | bytes 786436
  490.7 68.6 %collective-permute-start.9 = (bf16[192,256]{1,0:T(8,128)(2,1)S(1)}, bf16[192,256]{1,0:T(8,128)(2,1)S(1)}, u32[]{:S(2)}, u32[]{:S(2)}) collective-permute-start(bf16[192,256]{1,0:T(8,128)(2,1)S(1)} %copy-done.5), channel_id=1, source_target_pairs={{128,0},{129,1},{130,2},{131,3},{132,4},{133,5},{134,6},{135,7},{1... | collective-permute-start | bytes 294920 | tf_op jit(solution)/shard_map/ppermute | solution.py:100
  559.3 6.7 %collective-permute-start.8 = (bf16[192,256]{1,0:T(8,128)(2,1)S(1)}, bf16[192,256]{1,0:T(8,128)(2,1)S(1)}, u32[]{:S(2)}, u32[]{:S(2)}) collective-permute-start(bf16[192,256]{1,0:T(8,128)(2,1)S(1)} %get-tuple-element.274), channel_id=1, source_target_pairs={{0,128},{1,129},{2,130},{3,131},{4,132},{5,133},{6,134},{7,135},{8... | collective-permute-start | bytes 294920 | tf_op jit(solution)/shard_map/ppermute | solution.py:101
Sparse Core Ops, SparseCore 0:
  219.4 67.7 all-gather.2
  490.8 66.4 all-gather.4
